TPU v7x, 256 devices: a whole 4x4x8 slice. The times are simulated.
256 devices in a mesh: group: 4 (over y), shard: 16 (over x_hi, z), tensor: 4 (over x_lo, core).
Axes of the slice: x: 4 (x_hi: 2, x_lo: 2; x = x_hi * 2 + x_lo), y: 4, z: 8, core: 2. Of those that a mesh axis runs over, the one named last changes fastest.
Arguments:
- group_weights: bfloat16 [4, 8, 1024, 8704], P('group', None, None, ('shard', 'tensor')), may hold values from -6 to 6
- anchor: float32 [8, 1024, 16, 4, 136], P(None, ('group', 'shard'), None, 'tensor'), may hold values from -6 to 6
- momentum: float32 [8, 1024, 16, 4, 136], P(None, ('group', 'shard'), None, 'tensor'), may hold values from -6 to 6
- group_embedding: bfloat16 [4, 32000, 1024], P('group', 'shard', 'tensor'), may hold values from -6 to 6
- emb_anchor: float32 [32000, 1024], P('shard', 'tensor'), may hold values from -6 to 6
- emb_momentum: float32 [32000, 1024], P('shard', 'tensor'), may hold values from -6 to 6
- basis: float32 [1024, 64], P('tensor'), may hold values from -0.1875 to 0.1875
Outputs:
- new_weights: bfloat16 [8, 1024, 8704], P(None, None, ('shard', 'tensor'))
- new_anchor: float32 [8, 1024, 16, 4, 136], P(None, ('group', 'shard'), None, 'tensor')
- new_momentum: float32 [8, 1024, 16, 4, 136], P(None, ('group', 'shard'), None, 'tensor')
- new_embedding: bfloat16 [32000, 1024], P('shard', 'tensor')
- new_emb_anchor: float32 [32000, 1024], P('shard', 'tensor')
- new_emb_momentum: float32 [32000, 1024], P('shard', 'tensor')
All inputs are finite; a program needn't handle non-finite values.
Results may differ from a plain program's by a relative error of at most 0.012.
Values may be sent and summed in bfloat16 or wider, within the bound.
No kernel may reach another device: no remote copies, remote signals or barrier semaphores. Data moves between devices by JAX's collectives and lax.ppermute only.
A program may use at most 128 MiB of HBM per device.

v0:
```python
import jax
import jax.numpy as jnp
from jax import lax
from jax.sharding import PartitionSpec as P

outer_rate = 0.7
momentum_decay = 0.9


def per_device(group_weights, anchor, momentum, group_embedding, emb_anchor, emb_momentum, basis):
    groups = lax.axis_size("group")
    layers = group_weights.shape[1]
    width = group_weights.shape[2]
    block = group_weights.shape[3]
    local_weights = group_weights[0]
    part = lax.psum_scatter(
        local_weights.astype(jnp.float32).astype(jnp.bfloat16),
        "group",
        scatter_dimension=1,
        tiled=True,
    ).astype(jnp.float32)
    part = part.reshape(layers, part.shape[1], 1, 1, block)
    summed = lax.all_to_all(part, "shard", split_axis=1, concat_axis=2, tiled=True)
    delta = anchor - summed / groups
    moved = momentum_decay * momentum + delta
    stepped = anchor - outer_rate * (delta + momentum_decay * moved)
    stepped_half = stepped.astype(jnp.bfloat16)
    columns = lax.all_to_all(stepped_half, "shard", split_axis=2, concat_axis=1, tiled=True)
    whole = lax.all_gather(columns, "group", axis=1, tiled=True)
    new_weights = whole.reshape(layers, width, block)
    local_embedding = group_embedding[0].astype(jnp.float32)
    emb_sum = lax.psum(local_embedding.astype(jnp.bfloat16), "group").astype(jnp.float32)
    difference = emb_anchor - emb_sum / groups
    coef = lax.psum(jnp.dot(difference, basis, precision=lax.Precision.HIGHEST), "tensor")
    emb_delta = jnp.dot(coef, basis.T, precision=lax.Precision.HIGHEST)
    emb_moved = momentum_decay * emb_momentum + emb_delta
    emb_stepped = emb_anchor - outer_rate * (emb_delta + momentum_decay * emb_moved)
    return (new_weights, stepped, moved, emb_stepped.astype(jnp.bfloat16), emb_stepped, emb_moved)


def solution(mesh):
    return jax.shard_map(
        per_device,
        mesh=mesh,
        in_specs=(
            P("group", None, None, ("shard", "tensor")),
            P(None, ("group", "shard"), None, "tensor", None),
            P(None, ("group", "shard"), None, "tensor", None),
            P("group", "shard", "tensor"),
            P("shard", "tensor"),
            P("shard", "tensor"),
            P("tensor", None),
        ),
        out_specs=(
            P(None, None, ("shard", "tensor")),
            P(None, ("group", "shard"), None, "tensor", None),
            P(None, ("group", "shard"), None, "tensor", None),
            P("shard", "tensor"),
            P("shard", "tensor"),
            P("shard", "tensor"),
        ),
        check_vma=False,
    )
```

profile of v0, /device:TPU:1, one launch (start us, length us, event | category | flops | bytes accessed | tf_op | source)
XLA Modules:
  0.0 260.1 jit_solution(16609563485341192564)
XLA Ops:
  7.2 0.0 copy-start
  7.2 0.0 reduce-scatter.2.cloned.1.call-start
  7.2 6.8 %copy.20 = bf16[1,8,1024,136]{3,1,2,0:T(8,128)(2,1)} copy(bf16[1,8,1024,136]{2,3,1,0:T(8,128)(2,1)} %param.7) | data formatting | bytes 4456448 | tf_op args[0]
  14.0 0.0 reduce-scatter.2.cloned.1.call-update
  14.0 53.3 %reduce-scatter.2.cloned.1.call-done = bf16[8,256,136]{2,0,1:T(8,128)(2,1)} async-done(((bf16[8,1024,136]{2,0,1:T(8,128)(2,1)}), bf16[8,256,136]{2,0,1:T(8,128)(2,1)}) %reduce-scatter.2.cloned.1.call-update) | async-done | bytes 557072 | tf_op jit(solution)/shard_map/reduce_scatter | solution.py:16
  67.3 2.7 %bitcast_convert_fusion = f32[8,256,1,1,136]{4,0,3,2,1:T(8,128)} fusion(bf16[8,256,136]{2,0,1:T(8,128)(2,1)} %reduce-scatter.2.cloned.1.call-done), kind=kLoop, calls=%fused_computation.11 | loop fusion | flops 278528 | bytes 1671168 | tf_op jit(solution)/shard_map/reshape | solution.py:22
  70.0 9.2 %all-to-all-start = ((f32[8,256,1,1,136]{4,0,3,2,1:T(8,128)}), f32[8,256,1,1,136]{4,0,3,2,1:T(8,128)S(1)}, u32[]{:S(2)}, u32[]{:S(2)}) async-start(f32[8,256,1,1,136]{4,0,3,2,1:T(8,128)} %bitcast_convert_fusion), calls=%async_computation.1 | async-start | bytes 4194304 | tf_op jit(solution)/shard_map/all_to_all | solution.py:23
  79.3 0.0 all-reduce.3.cloned.1.call-start
  79.3 0.7 all-reduce.3.cloned.1.call-update
  80.0 48.4 %all-to-all-done = f32[8,256,1,1,136]{4,0,3,2,1:T(8,128)S(1)} async-done(((f32[8,256,1,1,136]{4,0,3,2,1:T(8,128)}), f32[8,256,1,1,136]{4,0,3,2,1:T(8,128)S(1)}, u32[]{:S(2)}, u32[]{:S(2)}) %all-to-all-start) | async-done | bytes 1114144 | tf_op jit(solution)/shard_map/all_to_all | solution.py:23
  128.5 0.0 copy-start.2
  128.5 0.0 copy-start.3
  128.5 0.7 copy_multiply_fusion.1
  129.2 0.9 copy-done.2
  130.1 0.6 copy-done.3
  130.7 5.1 %fusion.8 = (bf16[8,16,16,1,136]{4,1,2,0,3:T(8,128)(2,1)S(1)}, f32[8,16,16,1,136]{4,1,2,0,3:T(8,128)}, f32[8,16,16,1,136]{4,1,2,0,3:T(8,128)S(1)}) fusion(f32[8,16,16,1,136]{4,3,2,1,0:T(1,128)S(1)} %copy-done.2, f32[8,16,16,1,136]{4,1,2,0,3:T(8,128)S(1)} %bitcast.19, f32[8,16,16,1,136]{4,3,2,1,0:T(1,128)S(1)} %copy-done.3), kind=kLoop, calls=%fused_computation.15 | loop fusion | flops 2228224 | bytes 6127616 | tf_op jit(solution)/shard_map/convert_element_type | solution.py:27
  135.8 1.1 copy.25
  136.9 7.1 %all-to-all-start.1 = ((bf16[8,16,16,1,136]{4,1,0,3,2:T(8,128)(2,1)}), bf16[8,16,16,1,136]{4,1,0,3,2:T(8,128)(2,1)S(1)}, u32[]{:S(2)}, u32[]{:S(2)}) async-start(bf16[8,16,16,1,136]{4,1,0,3,2:T(8,128)(2,1)} %copy.25), calls=%async_computation.2 | async-start | bytes 2097152 | tf_op jit(solution)/shard_map/all_to_all | solution.py:28
  144.0 0.0 all-reduce.5.cloned.1.call-start
  144.1 0.0 all-reduce.3.cloned.1.call-done
  144.1 0.0 copy-done
  144.1 4.8 %fusion.1 = f32[2000,64]{0,1:T(8,128)} fusion(f32[256,64]{0,1:T(8,128)S(1)} %copy-done, f32[2000,256]{1,0:T(8,128)} %param.11, bf16[2000,256]{1,0:T(8,128)(2,1)} %all-reduce.3.cloned.1.call-done), kind=kOutput, calls=%fused_computation.6 | convolution fusion | flops 394752000 | bytes 3649536 | tf_op jit(solution)/shard_map/dot_general | solution.py:34
  148.9 0.0 all-reduce.5.cloned.1.call-update
  148.9 0.2 all-gather.2.cloned.1.call-start
  149.1 21.9 %all-to-all-done.1 = bf16[8,16,16,1,136]{4,1,0,3,2:T(8,128)(2,1)S(1)} async-done(((bf16[8,16,16,1,136]{4,1,0,3,2:T(8,128)(2,1)}), bf16[8,16,16,1,136]{4,1,0,3,2:T(8,128)(2,1)S(1)}, u32[]{:S(2)}, u32[]{:S(2)}) %all-to-all-start.1) | async-done | bytes 557088 | tf_op jit(solution)/shard_map/all_to_all | solution.py:28
  171.1 1.1 copy.26
  172.2 0.0 all-gather.2.cloned.1.call-update
  172.2 22.1 %all-reduce.5.cloned.1.call-done = f32[2000,64]{0,1:T(8,128)} async-done(((f32[2000,64]{0,1:T(8,128)}), f32[2000,64]{0,1:T(8,128)}) %all-reduce.5.cloned.1.call-update) | async-done | bytes 512016 | tf_op jit(solution)/shard_map/psum | solution.py:34
  194.3 0.0 copy-start.1
  194.3 6.9 %fusion.7 = (bf16[2000,256]{1,0:T(8,128)(2,1)}, f32[2000,256]{1,0:T(8,128)}, f32[2000,256]{1,0:T(8,128)}) fusion(f32[2000,256]{1,0:T(8,128)} %param.11, f32[2000,256]{1,0:T(8,128)} %param.12, f32[2000,64]{0,1:T(8,128)} %all-reduce.5.cloned.1.call-done, f32[256,64]{0,1:T(8,128)S(1)} %copy-done), kind=kOutput, calls=%fused_computation.14 | convolution fusion | flops 396800000 | bytes 9793536 | tf_op jit(solution)/shard_map/dot_general | solution.py:35
  201.3 0.0 copy-done.1
  201.3 3.7 %copy.28 = f32[8,16,16,1,136]{4,3,2,1,0:T(1,128)} copy(f32[8,16,16,1,136]{4,1,2,0,3:T(8,128)S(1)} %copy-done.1) | data formatting | bytes 2228224
  205.0 3.7 %copy.29 = f32[8,16,16,1,136]{4,3,2,1,0:T(1,128)} copy(f32[8,16,16,1,136]{4,1,2,0,3:T(8,128)S(1)} %get-tuple-element.23) | data formatting | bytes 2228224
  208.7 39.0 %all-gather.2.cloned.1.call-done = bf16[8,1024,1,1,136]{4,1,0,3,2:T(8,128)(2,1)} async-done(((bf16[8,256,1,1,136]{4,1,0,3,2:T(8,128)(2,1)}), bf16[8,1024,1,1,136]{4,1,0,3,2:T(8,128)(2,1)}) %all-gather.2.cloned.1.call-update) | async-done | bytes 2228240 | tf_op jit(solution)/shard_map/all_gather | solution.py:29
  247.7 5.9 %copy.27 = bf16[8,1024,136]{1,2,0:T(8,128)(2,1)} copy(bf16[8,1024,136]{2,1,0:T(8,128)(2,1)} %bitcast.20) | data formatting | bytes 4456448
Async XLA Ops:
  7.2 136.9 %copy-start = (f32[256,64]{0,1:T(8,128)S(1)}, f32[256,64]{0,1:T(8,128)}, u32[]{:S(2)}) copy-start(f32[256,64]{0,1:T(8,128)} %param.13) | copy-start | bytes 196612
  7.2 60.1 %reduce-scatter.2.cloned.1.call-start = ((), (), s32[]{:S(2)}) async-start(), calls=%async_computation.3 | async-start | bytes 5242880 | tf_op jit(solution)/shard_map/reduce_scatter | solution.py:16
  70.0 58.4 %all-to-all-start = ((f32[8,256,1,1,136]{4,0,3,2,1:T(8,128)}), f32[8,256,1,1,136]{4,0,3,2,1:T(8,128)S(1)}, u32[]{:S(2)}, u32[]{:S(2)}) async-start(f32[8,256,1,1,136]{4,0,3,2,1:T(8,128)} %bitcast_convert_fusion), calls=%async_computation.1 | async-start | bytes 4194304 | tf_op jit(solution)/shard_map/all_to_all | solution.py:23
  79.3 64.8 %all-reduce.3.cloned.1.call-start = ((), (), s32[]{:S(2)}) async-start(), calls=%async_computation.5 | async-start | bytes 2048000 | tf_op jit(solution)/shard_map/psum | solution.py:32
  128.5 1.6 copy-start.2
  128.5 2.3 copy-start.3
  136.9 34.2 %all-to-all-start.1 = ((bf16[8,16,16,1,136]{4,1,0,3,2:T(8,128)(2,1)}), bf16[8,16,16,1,136]{4,1,0,3,2:T(8,128)(2,1)S(1)}, u32[]{:S(2)}, u32[]{:S(2)}) async-start(bf16[8,16,16,1,136]{4,1,0,3,2:T(8,128)(2,1)} %copy.25), calls=%async_computation.2 | async-start | bytes 2097152 | tf_op jit(solution)/shard_map/all_to_all | solution.py:28
  144.0 50.3 %all-reduce.5.cloned.1.call-start = ((), (), s32[]{:S(2)}) async-start(), calls=%async_computation.6 | async-start | bytes 1048576 | tf_op jit(solution)/shard_map/psum | solution.py:34
  148.9 98.8 %all-gather.2.cloned.1.call-start = ((), (), s32[]{:S(2)}) async-start(), calls=%async_computation.4 | async-start | bytes 5242880 | tf_op jit(solution)/shard_map/all_gather | solution.py:29
  194.3 6.9 %copy-start.1 = (f32[8,16,16,1,136]{4,1,2,0,3:T(8,128)S(1)}, f32[8,16,16,1,136]{4,1,2,0,3:T(8,128)}, u32[]{:S(2)}) copy-start(f32[8,16,16,1,136]{4,1,2,0,3:T(8,128)} %get-tuple-element.22) | copy-start | bytes 3342340
Sparse Core Ops, SparseCore 0:
  14.1 53.1 reduce-scatter.1
  82.4 50.1 all-reduce.2
  149.0 45.2 all-reduce.4
  196.6 51.0 all-gather.1
where the time goes:
time: 261 us; the launch traced here: 260 us
  waiting for transfers between devices  186 us (71%)
  local copies, waits for them, and re-layouts  23.8 us (9%)
  starting transfers between devices  16.7 us (6%)
  between operations  13.8 us (5%)
  matrix products  11.7 us (4%)
  other arithmetic  8.55 us (3%)
    reduce_scatter x1, waiting for transfers between devices, per_device(): lax.psum_scatter(local_weights.astype(jnp.float32).astype(jnp.bfloat16),...  53.3 us
    all_to_all x1, waiting for transfers between devices, per_device(): lax.all_to_all(part, 'shard', split_axis=1, concat_axis=2, tiled=True)  48.4 us
    all_gather x1, waiting for transfers between devices, per_device(): whole = lax.all_gather(columns, 'group', axis=1, tiled=True)  39 us
    psum x1, waiting for transfers between devices, per_device(): lax.psum(jnp.dot(difference, basis, precision=lax.Precision.HIGHEST), 'te...  22.1 us
    all_to_all x1, waiting for transfers between devices, per_device(): lax.all_to_all(stepped_half, 'shard', split_axis=2, concat_axis=1, tiled=...  21.9 us
    unnamed x12, local copies, waits for them, and re-layouts  21.6 us
    all_to_all x1, starting transfers between devices, per_device(): lax.all_to_all(part, 'shard', split_axis=1, concat_axis=2, tiled=True)  9.24 us
    all_to_all x1, starting transfers between devices, per_device(): lax.all_to_all(stepped_half, 'shard', split_axis=2, concat_axis=1, tiled=...  7.1 us
  transfers between devices with their start and end apart: 6, of which 5 were waited for; matrix products, arithmetic and copies ran while one was open for 10% of the time, Pallas kernels for 0%

commit v1 on v0

--- a/solution.py
+++ b/solution.py
@@ -26,7 +26,9 @@
     stepped = anchor - outer_rate * (delta + momentum_decay * moved)
     stepped_half = stepped.astype(jnp.bfloat16)
     columns = lax.all_to_all(stepped_half, "shard", split_axis=2, concat_axis=1, tiled=True)
-    whole = lax.all_gather(columns, "group", axis=1, tiled=True)
+    whole = jnp.concatenate(
+        lax.all_to_all(jnp.stack([columns] * lax.axis_size("group")), "group", 0, 0), axis=1
+    )
     new_weights = whole.reshape(layers, width, block)
     local_embedding = group_embedding[0].astype(jnp.float32)
     emb_sum = lax.psum(local_embedding.astype(jnp.bfloat16), "group").astype(jnp.float32)

time: 261 us -> 285 us (1.092)
  blocking collectives: 0 us -> 57.8 us
  waiting for transfers between devices: 186 us -> 156 us
  starting transfers between devices: 16.7 us -> 10.3 us
  local copies, waits for them, and re-layouts: 23.8 us -> 27.1 us
    all_to_all x0 -> x1, blocking collectives: none -> 57.8 us  [per_device(): lax.all_to_all(part, 'shard', split_axis=1, concat_axis=2, tiled=True)]
    all_to_all x1, waiting for transfers between devices: 48.4 us -> 0.01 us  [per_device(): lax.all_to_all(jnp.stack([columns] * lax.axis_size('group')), 'group', 0, 0)]
    all_gather x1 -> x0, waiting for transfers between devices: 39 us -> none  [per_device(): whole = lax.all_gather(columns, 'group', axis=1, tiled=True)]
    psum x1, waiting for transfers between devices: 0.02 us -> 28.3 us  [per_device(): lax.psum(local_embedding.astype(jnp.bfloat16), 'group').astype(jnp.float32)]
    psum x1, waiting for transfers between devices: 22.1 us -> 48 us  [per_device(): lax.psum(jnp.dot(difference, basis, precision=lax.Precision.HIGHEST), 'te...]
    another operation x0 -> x3, local copies, waits for them, and re-layouts: none -> 7.15 us  [the longest x1 5.11 us: per_device(): new_weights = whole.reshape(layers, width, block)]
    unnamed x12 -> x13, local copies, waits for them, and re-layouts: 21.6 us -> 15.7 us
    all_to_all x1, starting transfers between devices: 9.24 us -> 3.62 us  [per_device(): lax.all_to_all(jnp.stack([columns] * lax.axis_size('group')), 'group', 0, 0)]
  transfers between devices with their start and end apart: 6 -> 5, of which waited for: 5 -> 4; matrix products, arithmetic and copies ran while one was open for 10% -> 7% of each run, Pallas kernels for 0% -> 0%
where the time goes in v1:
time: 285 us
  waiting for transfers between devices  156 us (55%)
  blocking collectives  57.8 us (20%)
  local copies, waits for them, and re-layouts  27.1 us (10%)
  between operations  13.8 us (5%)
  matrix products  11.7 us (4%)
  starting transfers between devices  10.3 us (4%)
  other arithmetic  7.91 us (3%)
    all_to_all x1, blocking collectives, per_device(): lax.all_to_all(part, 'shard', split_axis=1, concat_axis=2, tiled=True)  57.8 us
    reduce_scatter x1, waiting for transfers between devices, per_device(): lax.psum_scatter(local_weights.astype(jnp.float32).astype(jnp.bfloat16),...  53.3 us
    psum x1, waiting for transfers between devices, per_device(): lax.psum(jnp.dot(difference, basis, precision=lax.Precision.HIGHEST), 'te...  48 us
    psum x1, waiting for transfers between devices, per_device(): lax.psum(local_embedding.astype(jnp.bfloat16), 'group').astype(jnp.float32)  28.3 us
    all_to_all x1, waiting for transfers between devices, per_device(): lax.all_to_all(stepped_half, 'shard', split_axis=2, concat_axis=1, tiled=...  25.7 us
    unnamed x13, local copies, waits for them, and re-layouts  15.7 us
    dot_general x1, matrix products, per_device(): emb_delta = jnp.dot(coef, basis.T, precision=lax.Precision.HIGHEST)  6.94 us
    all_to_all x1, starting transfers between devices, per_device(): lax.all_to_all(stepped_half, 'shard', split_axis=2, concat_axis=1, tiled=...  6.37 us
  transfers between devices with their start and end apart: 5, of which 4 were waited for; matrix products, arithmetic and copies ran while one was open for 7% of the time, Pallas kernels for 0%

profile of v1, /device:TPU:1, one launch (start us, length us, event | category | flops | bytes accessed | tf_op | source)
XLA Modules:
  0.0 284.6 jit_solution(8560308159272836666)
XLA Ops:
  7.2 0.0 copy-start
  7.2 0.0 reduce-scatter.2.cloned.1.call-start
  7.2 6.8 %copy.30 = bf16[1,8,1024,136]{3,1,2,0:T(8,128)(2,1)} copy(bf16[1,8,1024,136]{2,3,1,0:T(8,128)(2,1)} %param.7) | data formatting | bytes 4456448 | tf_op args[0]
  14.0 0.0 reduce-scatter.2.cloned.1.call-update
  14.0 53.3 %reduce-scatter.2.cloned.1.call-done = bf16[8,256,136]{2,0,1:T(8,128)(2,1)} async-done(((bf16[8,1024,136]{2,0,1:T(8,128)(2,1)}), bf16[8,256,136]{2,0,1:T(8,128)(2,1)}) %reduce-scatter.2.cloned.1.call-update) | async-done | bytes 557072 | tf_op jit(solution)/shard_map/reduce_scatter | solution.py:16
  67.3 1.4 bitcast_convert_fusion
  68.7 57.8 %all_to_all.29 = f32[8,256,1,1,136]{4,0,3,2,1:T(8,128)S(1)} all-to-all(f32[8,256,1,1,136]{4,0,3,2,1:T(8,128)S(1)} %bitcast_convert_fusion), channel_id=1, replica_groups=mesh['group'=4,'shard'=16,'tensor'=4] {'shard'}, dimensions={1} | all-to-all | bytes 2228224 | tf_op jit(solution)/shard_map/all_to_all | solution.py:23
  126.4 0.0 copy-start.3
  126.5 0.0 copy-start.4
  126.5 0.7 copy_multiply_fusion.1
  127.2 0.8 copy-done.3
  128.0 0.6 copy-done.4
  128.7 5.8 %fusion.8 = (bf16[8,16,16,1,136]{4,1,2,0,3:T(8,128)(2,1)S(1)}, f32[8,16,16,1,136]{4,1,2,0,3:T(8,128)}, f32[8,16,16,1,136]{4,1,2,0,3:T(8,128)}) fusion(f32[8,16,16,1,136]{4,3,2,1,0:T(1,128)S(1)} %copy-done.3, f32[8,16,16,1,136]{4,1,2,0,3:T(8,128)S(1)} %bitcast.22, f32[8,16,16,1,136]{4,3,2,1,0:T(1,128)S(1)} %copy-done.4), kind=kLoop, calls=%fused_computation.15 | loop fusion | flops 2228224 | bytes 6127616 | tf_op jit(solution)/shard_map/convert_element_type | solution.py:27
  134.5 1.1 copy.35
  135.5 6.4 %all-to-all-start.1 = ((bf16[8,16,16,1,136]{4,1,0,3,2:T(8,128)(2,1)}), bf16[8,16,16,1,136]{4,1,0,3,2:T(8,128)(2,1)S(1)}, u32[]{:S(2)}, u32[]{:S(2)}) async-start(bf16[8,16,16,1,136]{4,1,0,3,2:T(8,128)(2,1)} %copy.35), calls=%async_computation.2 | async-start | bytes 2097152 | tf_op jit(solution)/shard_map/all_to_all | solution.py:28
  141.9 0.0 all-reduce.3.cloned.1.call-start
  142.0 0.7 all-reduce.3.cloned.1.call-update
  142.7 25.7 %all-to-all-done.1 = bf16[8,16,16,1,136]{4,1,0,3,2:T(8,128)(2,1)S(1)} async-done(((bf16[8,16,16,1,136]{4,1,0,3,2:T(8,128)(2,1)}), bf16[8,16,16,1,136]{4,1,0,3,2:T(8,128)(2,1)S(1)}, u32[]{:S(2)}, u32[]{:S(2)}) %all-to-all-start.1) | async-done | bytes 557088 | tf_op jit(solution)/shard_map/all_to_all | solution.py:28
  168.4 0.1 copy.36
  168.5 0.5 copy.37
  169.0 1.5 stack.10
  170.6 3.6 %all-to-all-start.2 = ((bf16[4,8,256,1,1,136]{2,5,1,4,3,0:T(8,128)(2,1)}), bf16[4,8,256,1,1,136]{2,5,1,4,3,0:T(8,128)(2,1)S(1)}, u32[]{:S(2)}, u32[]{:S(2)}) async-start(bf16[4,8,256,1,1,136]{2,5,1,4,3,0:T(8,128)(2,1)} %stack.10), calls=%async_computation.3 | async-start | bytes 4456448 | tf_op jit(solution)/shard_map/all_to_all | solution.py:30
  174.2 0.2 all-reduce.5.cloned.1.call-start
  174.4 28.3 %all-reduce.3.cloned.1.call-done = bf16[2000,256]{1,0:T(8,128)(2,1)} async-done(((bf16[2000,256]{1,0:T(8,128)(2,1)}), bf16[2000,256]{1,0:T(8,128)(2,1)}) %all-reduce.3.cloned.1.call-update) | async-done | bytes 1024016 | tf_op jit(solution)/shard_map/psum | solution.py:34
  202.7 0.0 copy-done
  202.7 4.8 %fusion.1 = f32[2000,64]{0,1:T(8,128)} fusion(f32[256,64]{0,1:T(8,128)S(1)} %copy-done, f32[2000,256]{1,0:T(8,128)} %param.11, bf16[2000,256]{1,0:T(8,128)(2,1)} %all-reduce.3.cloned.1.call-done), kind=kOutput, calls=%fused_computation.6 | convolution fusion | flops 394752000 | bytes 3649536 | tf_op jit(solution)/shard_map/dot_general | solution.py:36
  207.5 0.0 all-reduce.5.cloned.1.call-update
  207.5 48.0 %all-reduce.5.cloned.1.call-done = f32[2000,64]{0,1:T(8,128)} async-done(((f32[2000,64]{0,1:T(8,128)}), f32[2000,64]{0,1:T(8,128)}) %all-reduce.5.cloned.1.call-update) | async-done | bytes 512016 | tf_op jit(solution)/shard_map/psum | solution.py:36
  255.5 0.0 copy-start.2
  255.5 6.9 %fusion.7 = (bf16[2000,256]{1,0:T(8,128)(2,1)}, f32[2000,256]{1,0:T(8,128)}, f32[2000,256]{1,0:T(8,128)}) fusion(f32[2000,256]{1,0:T(8,128)} %param.11, f32[2000,256]{1,0:T(8,128)} %param.12, f32[2000,64]{0,1:T(8,128)} %all-reduce.5.cloned.1.call-done, f32[256,64]{0,1:T(8,128)S(1)} %copy-done), kind=kOutput, calls=%fused_computation.14 | convolution fusion | flops 396800000 | bytes 9793536 | tf_op jit(solution)/shard_map/dot_general | solution.py:37
  262.4 0.0 copy-done.2
  262.4 0.0 copy-start.1
  262.4 3.7 %copy.39 = f32[8,16,16,1,136]{4,3,2,1,0:T(1,128)} copy(f32[8,16,16,1,136]{4,1,2,0,3:T(8,128)S(1)} %copy-done.2) | data formatting | bytes 2228224
  266.1 0.0 copy-done.1
  266.1 3.7 %copy.40 = f32[8,16,16,1,136]{4,3,2,1,0:T(1,128)} copy(f32[8,16,16,1,136]{4,1,2,0,3:T(8,128)S(1)} %copy-done.1) | data formatting | bytes 2228224
  269.9 0.0 all-to-all-done.2
  269.9 3.1 %copy.38 = bf16[8,4,256,1,1,136]{2,1,5,0,4,3:T(4,128)(2,1)} copy(bf16[8,4,256,1,1,136]{2,5,0,4,3,1:T(8,128)(2,1)S(1)} %bitcast.21) | data formatting | bytes 4456448 | tf_op jit(solution)/shard_map/reshape | solution.py:29
  273.0 5.1 %reshape_reshape.3 = bf16[8,1024,136]{1,2,0:T(8,128)(2,1)} reshape(bf16[8,4,256,1,1,136]{2,1,5,0,4,3:T(4,128)(2,1)} %copy.38) | data formatting | bytes 4456448 | tf_op jit(solution)/shard_map/reshape;reshape | solution.py:32
Async XLA Ops:
  7.2 195.5 %copy-start = (f32[256,64]{0,1:T(8,128)S(1)}, f32[256,64]{0,1:T(8,128)}, u32[]{:S(2)}) copy-start(f32[256,64]{0,1:T(8,128)} %param.13) | copy-start | bytes 196612
  7.2 60.1 %reduce-scatter.2.cloned.1.call-start = ((), (), s32[]{:S(2)}) async-start(), calls=%async_computation.4 | async-start | bytes 5242880 | tf_op jit(solution)/shard_map/reduce_scatter | solution.py:16
  126.4 1.6 copy-start.3
  126.5 2.2 copy-start.4
  135.5 32.9 %all-to-all-start.1 = ((bf16[8,16,16,1,136]{4,1,0,3,2:T(8,128)(2,1)}), bf16[8,16,16,1,136]{4,1,0,3,2:T(8,128)(2,1)S(1)}, u32[]{:S(2)}, u32[]{:S(2)}) async-start(bf16[8,16,16,1,136]{4,1,0,3,2:T(8,128)(2,1)} %copy.35), calls=%async_computation.2 | async-start | bytes 2097152 | tf_op jit(solution)/shard_map/all_to_all | solution.py:28
  141.9 60.8 %all-reduce.3.cloned.1.call-start = ((), (), s32[]{:S(2)}) async-start(), calls=%async_computation.5 | async-start | bytes 2048000 | tf_op jit(solution)/shard_map/psum | solution.py:34
  170.6 99.3 %all-to-all-start.2 = ((bf16[4,8,256,1,1,136]{2,5,1,4,3,0:T(8,128)(2,1)}), bf16[4,8,256,1,1,136]{2,5,1,4,3,0:T(8,128)(2,1)S(1)}, u32[]{:S(2)}, u32[]{:S(2)}) async-start(bf16[4,8,256,1,1,136]{2,5,1,4,3,0:T(8,128)(2,1)} %stack.10), calls=%async_computation.3 | async-start | bytes 4456448 | tf_op jit(solution)/shard_map/all_to_all | solution.py:30
  174.2 81.3 %all-reduce.5.cloned.1.call-start = ((), (), s32[]{:S(2)}) async-start(), calls=%async_computation.6 | async-start | bytes 1048576 | tf_op jit(solution)/shard_map/psum | solution.py:36
  255.5 6.9 %copy-start.2 = (f32[8,16,16,1,136]{4,1,2,0,3:T(8,128)S(1)}, f32[8,16,16,1,136]{4,1,2,0,3:T(8,128)}, u32[]{:S(2)}) copy-start(f32[8,16,16,1,136]{4,1,2,0,3:T(8,128)} %get-tuple-element.28) | copy-start | bytes 3342340
  262.4 3.7 %copy-start.1 = (f32[8,16,16,1,136]{4,1,2,0,3:T(8,128)S(1)}, f32[8,16,16,1,136]{4,1,2,0,3:T(8,128)}, u32[]{:S(2)}) copy-start(f32[8,16,16,1,136]{4,1,2,0,3:T(8,128)} %get-tuple-element.29) | copy-start | bytes 3342340
Sparse Core Ops, SparseCore 0:
  14.1 53.1 reduce-scatter.1
  145.1 57.5 all-reduce.2
  207.6 47.7 all-reduce.4
